TPU v7x, 32 devices: a whole 2x2x4 slice. The times are simulated.
32 devices in a mesh: req: 16 (over z, x, core), kv: 2 (over y).
Axes of the slice: x: 2, y: 2, z: 4, core: 2. Of those that a mesh axis runs over, the one named last changes fastest.
Arguments:
- hidden: bfloat16 [32, 256, 1024], P('req', 'kv'), may hold values from -6 to 6
- queries: bfloat16 [32, 256, 1024], P('req', 'kv'), may hold values from -24 to 24
- span_kv: bfloat16 [32, 256, 8, 128], P('req', 'kv'), may hold values from -48 to 48
- cache: bfloat16 [32, 2048, 8, 128], P('req', 'kv'), may hold values from -48 to 48
- req_order: int32 [32], replicated, may hold values from 0 to 31, each once
- cached_len: int32 [32], replicated, may hold values from 8 to 2048, as said below
- out_weight: bfloat16 [1024, 1024], replicated, may hold values from -0.1875 to 0.1875
- norm_gain: float32 [1024], replicated, may hold values from 0.1 to 1.9
- expert_ids: int32 [8192, 8], P(('req', 'kv')), may hold values from 0 to 15, all different within a row; in each aligned block of 256 rows (0 to 255, 256 to 511, ...) at most 256 rows name the same one
- expert_weights: float32 [8192, 8], P(('req', 'kv')), may hold values from 0.05 to 0.5
- w_experts: bfloat16 [16, 3, 1024, 512], P('req', None, None, 'kv'), may hold values from -0.25 to 0.25
- block_map: int32 [32, 128], P('req'), may hold values from 0 to 4095, as said below
Outputs:
- layer_out: bfloat16 [32, 256, 1024], P('req', 'kv')
- decode_pool: bfloat16 [4096, 8, 16, 128], P('req', 'kv')
Inputs may be any that keep to these rules, and one draw needn't show every extreme that they name: `cached_len`: some request fills its cache. `block_map`: a permutation of the 4096 pool pages; pool page s belongs to req index s // 256; the pages that one kv index holds of the slots of one req index (positions of its cache share) go to every req index equally often. `expert_ids`: in the rows of one device no expert is named more than 256 times.
All inputs are finite; a program needn't handle non-finite values.
Results may differ from a plain program's by a relative error of at most 0.023.
Values may be sent and summed in bfloat16 or wider, within the bound.
No kernel may reach another device: no remote copies, remote signals or barrier semaphores. Data moves between devices by JAX's collectives and lax.ppermute only.
A program may use at most 128 MiB of HBM per device.

v0:
```python
import math
import jax
import jax.numpy as jnp
from jax import lax
from jax.sharding import PartitionSpec as P

BLOCK = 16


def lookup_lengths(req_order, cached_len, count):
    start = lax.axis_index("req") * count
    mine = lax.dynamic_slice_in_dim(req_order, start, count)
    match = mine[:, None] == jnp.arange(cached_len.shape[0], dtype=jnp.int32)[None, :]
    return jnp.sum(jnp.where(match, cached_len[None, :], 0), axis=1)


def score_block(query_rows, cache_rows, span_rows):
    span_count, group_count, width = query_rows.shape
    head_dim = cache_rows.shape[-1] // 2
    per_group = width // head_dim
    query_split = query_rows.reshape(span_count, group_count, per_group, head_dim)
    key_rows = jnp.concatenate([cache_rows[..., :head_dim], span_rows[..., :head_dim]], axis=0)
    value_rows = jnp.concatenate([cache_rows[..., head_dim:], span_rows[..., head_dim:]], axis=0)
    scores = jnp.einsum(
        "igsd,pgd->gsip", query_split, key_rows, preferred_element_type=jnp.float32
    ) * (1.0 / math.sqrt(head_dim))
    return (scores, value_rows)


def soft_weights(scores, allowed, value_rows):
    masked = jnp.where(allowed, scores, -1e30)
    row_max = jnp.max(masked, axis=-1, keepdims=True)
    probability = jnp.where(allowed, jnp.exp(masked - row_max), 0.0)
    prob_sum = jnp.sum(probability, axis=-1)
    weighted = jnp.einsum(
        "gsip,pgd->igsd",
        probability.astype(jnp.bfloat16),
        value_rows,
        preferred_element_type=jnp.float32,
    )
    return (weighted, jnp.transpose(row_max[..., 0], (2, 0, 1)), jnp.transpose(prob_sum, (2, 0, 1)))


def whole_request(operands):
    query_rows, cache_rows, span_rows, length = operands
    scores, value_rows = score_block(query_rows, cache_rows, span_rows)
    cached = cache_rows.shape[0]
    position = jnp.arange(scores.shape[-1])[None, :]
    query_pos = jnp.arange(query_rows.shape[0])[:, None]
    allowed = jnp.where(position < cached, position < length, position - cached <= query_pos)
    weighted, row_max, prob_sum = soft_weights(scores, allowed, value_rows)
    result = weighted / prob_sum[..., None]
    return result.reshape(query_rows.shape).astype(jnp.bfloat16)


def place_pages(page_rows, slot_numbers, slots_dev):
    owner_index = slot_numbers // slots_dev
    arrangement = jnp.argsort(owner_index, stable=True)
    return (page_rows[arrangement], (slot_numbers % slots_dev)[arrangement])


def body(
    hidden,
    queries,
    span_kv,
    cache,
    req_order,
    cached_len,
    out_weight,
    norm_gain,
    expert_ids,
    expert_weights,
    w_experts,
    block_map,
):
    local_reqs, local_tokens, width_model = hidden.shape
    row_count = local_reqs * local_tokens
    req_count = lax.axis_size("req")
    kv_count = lax.axis_size("kv")
    kv_heads = span_kv.shape[2]
    head_pair = span_kv.shape[3]
    group_width = queries.shape[2] // kv_heads
    group_count = kv_heads // kv_count
    slots_dev = local_reqs * block_map.shape[1]
    lengths = lookup_lengths(req_order, cached_len, local_reqs)
    queries_grouped = queries.reshape(local_reqs, local_tokens, kv_heads, group_width)
    cache_heads, span_heads, query_heads = (
        lax.all_to_all(cache, "kv", split_axis=2, concat_axis=1, tiled=True),
        lax.all_to_all(span_kv, "kv", split_axis=2, concat_axis=1, tiled=True),
        lax.all_to_all(queries_grouped, "kv", split_axis=2, concat_axis=1, tiled=True),
    )
    attn_heads = lax.map(whole_request, (query_heads, cache_heads, span_heads, lengths))
    attn = lax.all_to_all(attn_heads, "kv", split_axis=1, concat_axis=2, tiled=True).reshape(
        row_count, kv_heads * group_width
    )
    page_total = block_map.shape[1]
    visible = jnp.arange(cache_heads.shape[1])[None, :] < lengths[:, None]
    visible_cache = jnp.where(visible[:, :, None, None], cache_heads, jnp.zeros((), jnp.bfloat16))
    page_rows = (
        visible_cache.reshape(local_reqs, page_total, BLOCK, group_count, head_pair)
        .transpose(0, 1, 3, 2, 4)
        .reshape(local_reqs * page_total, group_count, BLOCK, head_pair)
    )
    sorted_pages, local_slot = place_pages(page_rows, block_map.reshape(-1), slots_dev)
    per_owner = sorted_pages.shape[0] // req_count
    outgoing = sorted_pages.reshape(req_count, per_owner, group_count, BLOCK, head_pair)
    arrived, where_to = (
        lax.all_to_all(outgoing, "req", split_axis=0, concat_axis=0, tiled=True),
        lax.all_to_all(
            local_slot.reshape(req_count, per_owner), "req", split_axis=0, concat_axis=0, tiled=True
        ),
    )
    decode_pool = (
        jnp.zeros((slots_dev, group_count, BLOCK, head_pair), jnp.bfloat16)
        .at[where_to.reshape(-1)]
        .set(arrived.reshape(-1, group_count, BLOCK, head_pair))
    )
    residual = hidden.reshape(row_count, width_model).astype(jnp.float32) + jnp.dot(
        attn, out_weight, preferred_element_type=jnp.float32
    )
    inverse_rms = lax.rsqrt(jnp.mean(residual * residual, axis=-1, keepdims=True) + 1e-05)
    normed = (residual * inverse_rms * norm_gain).astype(jnp.bfloat16)
    top_count = expert_ids.shape[1]
    exp_dev = w_experts.shape[0]
    experts = exp_dev * req_count
    capacity = min(row_count, 2 * row_count * top_count // experts)
    chosen = expert_ids.reshape(-1)
    onehot = (chosen[:, None] == jnp.arange(experts, dtype=jnp.int32)[None, :]).astype(jnp.int32)
    slot_rank = jnp.sum(onehot * (jnp.cumsum(onehot, axis=0) - 1), axis=1)
    target = chosen * capacity + slot_rank
    source_row = jnp.arange(chosen.shape[0]) // top_count
    buffer = (
        jnp.zeros((experts * capacity, width_model), jnp.bfloat16)
        .at[target]
        .set(normed[source_row])
        .reshape(experts, capacity, width_model)
    )
    full_weights = lax.all_gather(w_experts, "kv", axis=3, tiled=True)
    slot_block = lax.all_to_all(buffer, "req", split_axis=0, concat_axis=0, tiled=True)
    source_count = slot_block.shape[0] // exp_dev
    grouped = slot_block.reshape(source_count, exp_dev, slot_block.shape[1], width_model)
    gate_act = jnp.einsum(
        "sejd,edf->sejf", grouped, full_weights[:, 0], preferred_element_type=jnp.float32
    )
    up_act = jnp.einsum(
        "sejd,edf->sejf", grouped, full_weights[:, 1], preferred_element_type=jnp.float32
    )
    activated = (jax.nn.silu(gate_act) * up_act).astype(jnp.bfloat16)
    expert_out = jnp.einsum(
        "sejf,edf->sejd", activated, full_weights[:, 2], preferred_element_type=jnp.float32
    ).astype(jnp.bfloat16)
    returned = lax.all_to_all(
        expert_out.reshape(slot_block.shape), "req", split_axis=0, concat_axis=0, tiled=True
    )
    picked = returned.reshape(experts * capacity, width_model)[target].reshape(
        row_count, top_count, width_model
    )
    expert_sum = jnp.sum(expert_weights[..., None] * picked.astype(jnp.float32), axis=1)
    layer_out = (
        (residual + expert_sum).astype(jnp.bfloat16).reshape(local_reqs, local_tokens, width_model)
    )
    return (layer_out, decode_pool)


def solution(mesh):
    return jax.shard_map(
        body,
        mesh=mesh,
        in_specs=(
            P("req", "kv", None),
            P("req", "kv", None),
            P("req", "kv", None, None),
            P("req", "kv", None, None),
            P(),
            P(),
            P(),
            P(),
            P(("req", "kv"), None),
            P(("req", "kv"), None),
            P("req", None, None, "kv"),
            P("req", None),
        ),
        out_specs=(P("req", "kv", None), P("req", "kv", None, None)),
        check_vma=False,
    )
```

profile of v0, /device:TPU:11, one launch (start us, length us, event | category | flops | bytes accessed | tf_op | source)
XLA Modules:
  0.0 748.4 jit_solution(12969157909613193286)
XLA Ops:
  7.2 2.1 copy.81
  9.3 3.5 all-to-all-start.1
  12.8 1.3 copy.83
  14.1 0.8 copy.84
  14.9 5.2 all-to-all-done.1
  20.1 3.5 all-to-all-start.2
  24.0 5.0 copy.78
  29.0 1.0 all-to-all-done.2
  30.1 5.6 all-to-all-start
  35.7 4.5 reduce-window.6
  41.8 3.2 sort.17
  47.7 1.1 copy.82
  48.8 2.2 all_to_all.74
  51.0 1.0 copy.86
  52.0 28.7 %all-to-all-done = bf16[2,1024,8,128]{3,1,0,2:T(8,128)(2,1)} async-done(((bf16[2,1024,8,128]{3,1,0,2:T(8,128)(2,1)}), bf16[2,1024,8,128]{3,1,0,2:T(8,128)(2,1)}, u32[]{:S(2)}, u32[]{:S(2)}) %all-to-all-start) | async-done | bytes 4194336 | tf_op jit(solution)/shard_map/all_to_all | solution.py:88
  80.7 4.6 copy.80
  85.3 104.1 %while.12 = (s32[]{:T(128)}, bf16[2,256,4,128]{3,2,0,1:T(4,128)(2,1)}, bf16[2,2048,4,128]{3,1,2,0:T(8,128)(2,1)}, bf16[2,256,4,128]{1,3,2,0:T(8,128)(2,1)}, s32[...) while((s32[]{:T(128)}, bf16[2,256,4,128]{3,2,0,1:T(4,128)(2,1)}, ...), condition=%wide.region_4.5_spmd, body=%wide.region_1.4_spmd.sunk | while | flops 1251877888 | bytes 80653984 | solution.py:92
  85.3 3.0 constant_dynamic-slice_fusion.5
  88.3 4.0 copy.115
  92.3 2.8 fusion.64
  95.8 0.7 constant_dynamic-slice_fusion.4
  96.5 1.1 copy.114
  97.6 9.2 %fusion.65 = f32[4,2304,256,2]{2,1,3,0:T(8,128)} fusion(bf16[256,4,2,64]{0,3,2,1:T(8,128)(2,1)S(1)} %bitcast.190, bf16[256,4,64]{0,2,1:T(8,128)(2,1)} %get-tuple-element.183, bf16[2048,4,64]{0,2,1:T(8,128)(2,1)} %get-tuple-element.184), kind=kOutput, calls=%fused_computation.24.clone.1 | convolution fusion | flops 606339072 | bytes 20316160 | tf_op jit(solution)/shard_map/while/body/eval_jaxpr/igsd,pgd->gsip/dot_general | solution.py:24
  106.9 1.2 dynamic_slice.41
  108.7 2.7 fusion.66
  111.4 19.4 %fusion.67 = (f32[4,2,256]{2,1,0:T(2,128)S(1)}, bf16[4,2,256,2304]{2,3,1,0:T(8,128)(2,1)}) fusion(f32[4,2304,256,2]{2,1,3,0:T(8,128)} %fusion.65, pred[256,2304]{0,1:T(8,128)(4,1)} %fusion.66), kind=kOutput, calls=%fused_computation.99.clone.1 | output fusion | flops 37751040 | bytes 28909568 | tf_op jit(solution)/shard_map/while/body/eval_jaxpr/sub | solution.py:33
  130.9 5.5 fusion.68
  136.5 0.8 constant_dynamic-update-slice_fusion.2
  137.3 3.0 constant_dynamic-slice_fusion.5
  140.4 4.0 copy.115
  144.4 2.8 fusion.64
  147.9 0.7 constant_dynamic-slice_fusion.4
  148.6 1.1 copy.114
  149.7 9.2 %fusion.65 = f32[4,2304,256,2]{2,1,3,0:T(8,128)} fusion(bf16[256,4,2,64]{0,3,2,1:T(8,128)(2,1)S(1)} %bitcast.190, bf16[256,4,64]{0,2,1:T(8,128)(2,1)} %get-tuple-element.183, bf16[2048,4,64]{0,2,1:T(8,128)(2,1)} %get-tuple-element.184), kind=kOutput, calls=%fused_computation.24.clone.1 | convolution fusion | flops 606339072 | bytes 20316160 | tf_op jit(solution)/shard_map/while/body/eval_jaxpr/igsd,pgd->gsip/dot_general | solution.py:24
  158.9 1.2 dynamic_slice.41
  160.8 2.7 fusion.66
  163.5 19.4 %fusion.67 = (f32[4,2,256]{2,1,0:T(2,128)S(1)}, bf16[4,2,256,2304]{2,3,1,0:T(8,128)(2,1)}) fusion(f32[4,2304,256,2]{2,1,3,0:T(8,128)} %fusion.65, pred[256,2304]{0,1:T(8,128)(4,1)} %fusion.66), kind=kOutput, calls=%fused_computation.99.clone.1 | output fusion | flops 37751040 | bytes 28909568 | tf_op jit(solution)/shard_map/while/body/eval_jaxpr/sub | solution.py:33
  182.9 5.5 fusion.68
  188.6 0.8 constant_dynamic-update-slice_fusion.2
  189.4 3.6 all-to-all-start.3
  193.1 1.9 gather_fusion.1
  196.4 2.0 all-to-all-done.3
  198.4 10.7 %all-to-all-start.6 = ((s32[16,1,16]{2,1,0:T(1,128)}), s32[16,1,16]{2,1,0:T(1,128)S(1)}, u32[]{:S(2)}, u32[]{:S(2)}) async-start(s32[16,1,16]{2,1,0:T(1,128)} %all_to_all.84), calls=%async_computation.6 | async-start | bytes 16384 | tf_op jit(solution)/shard_map/all_to_all | solution.py:109
  209.3 1.2 reshape.267
  210.5 2.0 multiply_reduce_fusion
  212.5 0.9 multiply_convert_fusion
  213.5 33.0 %scatter_custom_fusion = bf16[4096,1024]{1,0:T(8,128)(2,1)} fusion(s32[2048]{0:T(1024)S(1)} %bitcast.205, bf16[256,1024]{1,0:T(8,128)(2,1)} %multiply_convert_fusion, s32[2048]{0:T(1024)S(1)} %broadcast_clamp_fusion.1, bf16[]{:T(256)} %constant.114.clone.1), kind=kCustom, calls=%fused_computation.49 | custom fusion | bytes 8389120 | tf_op jit(solution)/shard_map/scatter | solution.py:135
  246.4 6.4 all-to-all-start.4
  253.5 2.6 select_bitcast_fusion
  256.1 3.3 copy.96
  259.4 5.2 gather_fusion.2
  264.6 170.4 %all-to-all-done.4 = bf16[16,256,1024]{2,1,0:T(8,128)(2,1)} async-done(((bf16[16,256,1024]{2,1,0:T(8,128)(2,1)}), bf16[16,256,1024]{2,1,0:T(8,128)(2,1)}, u32[]{:S(2)}, u32[]{:S(2)}) %all-to-all-start.4) | async-done | bytes 8388640 | tf_op jit(solution)/shard_map/all_to_all | solution.py:139
  435.0 4.9 all-to-all-start.7
  440.6 46.2 %all-gather.2.cloned.1.call-done = bf16[1,3,1024,512]{3,2,1,0:T(8,128)(2,1)} async-done(((bf16[1,3,1024,256]{3,2,1,0:T(8,128)(2,1)}), bf16[1,3,1024,512]{3,2,1,0:T(8,128)(2,1)}) %all-gather.2.cloned.1.call-update) | async-done | bytes 3145744 | tf_op jit(solution)/shard_map/all_gather | solution.py:138
  486.8 11.4 %fusion.38 = f32[16,256,512]{2,1,0:T(8,128)} fusion(bf16[16,256,1024]{2,1,0:T(8,128)(2,1)} %all-to-all-done.4, bf16[1,3,1024,512]{3,2,1,0:T(8,128)(2,1)} %all-gather.2.cloned.1.call-done), kind=kOutput, calls=%fused_computation.58 | convolution fusion | flops 4294967296 | bytes 17825792 | tf_op jit(solution)/shard_map/sejd,edf->sejf/dot_general | solution.py:142
  498.2 16.0 %convolution_convert_fusion = bf16[16,256,1024]{2,1,0:T(8,128)(2,1)} fusion(f32[16,256,512]{2,1,0:T(8,128)} %fusion.38, bf16[16,256,1024]{2,1,0:T(8,128)(2,1)} %all-to-all-done.4, bf16[1,3,1024,512]{3,2,1,0:T(8,128)(2,1)} %all-gather.2.cloned.1.call-done), kind=kOutput, calls=%fused_computation.47 | convolution fusion | flops 8606711808 | bytes 27262976 | tf_op jit(solution)/shard_map/sejf,edf->sejd/dot_general | solution.py:149
  514.2 18.2 %all-to-all-done.7 = bf16[16,16,4,16,128]{4,3,2,1,0:T(8,128)(2,1)} async-done(((bf16[16,16,4,16,128]{4,3,2,1,0:T(8,128)(2,1)}), bf16[16,16,4,16,128]{4,3,2,1,0:T(8,128)(2,1)}, u32[]{:S(2)}, u32[]{:S(2)}) %all-to-all-start.7) | async-done | bytes 4194336 | tf_op jit(solution)/shard_map/all_to_all | solution.py:108
  532.4 5.3 all-to-all-start.5
  539.1 3.1 broadcast_in_dim.106
  542.2 33.5 %scatter_fusion = bf16[256,4,16,128]{3,2,1,0:T(8,128)(2,1)} fusion(bf16[256,4,16,128]{3,2,1,0:T(8,128)(2,1)} %broadcast_in_dim.106, s32[256]{0:T(256)S(1)} %bitcast.209, bf16[256,4,16,128]{3,2,1,0:T(8,128)(2,1)} %bitcast.57), kind=kCustom, calls=%fused_computation.5 | custom fusion | bytes 12583936 | tf_op jit(solution)/shard_map/scatter | solution.py:116
  575.7 144.2 %all-to-all-done.5 = bf16[16,256,1024]{2,1,0:T(8,128)(2,1)} async-done(((bf16[16,256,1024]{2,1,0:T(8,128)(2,1)}), bf16[16,256,1024]{2,1,0:T(8,128)(2,1)}, u32[]{:S(2)}, u32[]{:S(2)}) %all-to-all-start.5) | async-done | bytes 8388640 | tf_op jit(solution)/shard_map/all_to_all | solution.py:152
  719.9 15.5 %gather_fusion = bf16[2048,1024]{1,0:T(8,128)(2,1)} fusion(bf16[4096,1024]{1,0:T(8,128)(2,1)} %bitcast.46, s32[2048]{0:T(1024)S(1)} %broadcast_clamp_fusion), kind=kCustom, calls=%fused_computation.1 | custom fusion | bytes 8396800 | tf_op jit(solution)/shard_map/gather | solution.py:155
  735.3 4.8 fusion.26
  740.1 1.0 add_convert_fusion
  (73 shorter events, 12.0 us)
Async XLA Ops:
  7.2 203.3 %copy-start = (bf16[1024,1024]{1,0:T(8,128)(2,1)S(1)}, bf16[1024,1024]{1,0:T(8,128)(2,1)}, u32[]{:S(2)}) copy-start(bf16[1024,1024]{1,0:T(8,128)(2,1)} %param.20) | copy-start | bytes 6291460
  7.2 16.5 %copy-start.4 = (s32[256,8]{0,1:T(8,128)S(1)}, s32[256,8]{0,1:T(8,128)}, u32[]{:S(2)}) copy-start(s32[256,8]{0,1:T(8,128)} %param.22) | copy-start | bytes 24580
  9.3 10.9 %all-to-all-start.1 = ((bf16[2,128,8,128]{3,1,0,2:T(8,128)(2,1)}), bf16[2,128,8,128]{3,1,0,2:T(8,128)(2,1)S(1)}, u32[]{:S(2)}, u32[]{:S(2)}) async-start(bf16[2,128,8,128]{3,1,0,2:T(8,128)(2,1)} %copy.81), calls=%async_computation.1 | async-start | bytes 1048576 | tf_op jit(solution)/shard_map/all_to_all | solution.py:89
  20.1 9.9 %all-to-all-start.2 = ((bf16[2,128,8,128]{1,3,0,2:T(8,128)(2,1)}), bf16[2,128,8,128]{1,3,0,2:T(8,128)(2,1)S(1)}, u32[]{:S(2)}, u32[]{:S(2)}) async-start(bf16[2,128,8,128]{1,3,0,2:T(8,128)(2,1)} %copy.84), calls=%async_computation.2 | async-start | bytes 1048576 | tf_op jit(solution)/shard_map/all_to_all | solution.py:90
  29.0 12.1 %copy-start.10 = (s32[32]{0:T(128)S(1)}, s32[32]{0:T(128)}, u32[]{:S(2)}) copy-start(s32[32]{0:T(128)} %param.18) | copy-start | bytes 388
  29.0 12.2 %copy-start.9 = (s32[2,128]{1,0:T(2,128)S(1)}, s32[2,128]{1,0:T(2,128)}, u32[]{:S(2)}) copy-start(s32[2,128]{1,0:T(2,128)} %param.25) | copy-start | bytes 3076
  29.0 16.0 %copy-start.11 = (s32[32]{0:T(128)S(1)}, s32[32]{0:T(128)}, u32[]{:S(2)}) copy-start(s32[32]{0:T(128)} %param.19) | copy-start | bytes 388
  30.1 50.6 %all-to-all-start = ((bf16[2,1024,8,128]{3,1,0,2:T(8,128)(2,1)}), bf16[2,1024,8,128]{3,1,0,2:T(8,128)(2,1)}, u32[]{:S(2)}, u32[]{:S(2)}) async-start(bf16[2,1024,8,128]{3,1,0,2:T(8,128)(2,1)} %copy.78), calls=%async_computation | async-start | bytes 8388608 | tf_op jit(solution)/shard_map/all_to_all | solution.py:88
  85.3 107.8 %copy-start.8 = (s32[256]{0:T(256)S(1)}, s32[256]{0:T(256)}, u32[]{:S(2)}) copy-start(s32[256]{0:T(256)} %compare_select_fusion.3) | copy-start | bytes 3076
  85.3 107.8 %copy-start.1 = (s32[256]{0:T(256)S(1)}, s32[256]{0:T(256)}, u32[]{:S(2)}) copy-start(s32[256]{0:T(256)} %get-tuple-element.133) | copy-start | bytes 3076
  92.3 2.8 copy-start.2
  92.3 3.5 copy-start.3
  144.4 2.8 copy-start.2
  144.4 3.5 copy-start.3
  189.4 23.1 %copy-start.7 = (f32[1024]{0:T(1024)S(1)}, f32[1024]{0:T(1024)}, u32[]{:S(2)}) copy-start(f32[1024]{0:T(1024)} %param.21) | copy-start | bytes 12292
  189.4 9.0 %all-to-all-start.3 = ((bf16[2,256,4,128]{3,2,0,1:T(4,128)(2,1)}), bf16[2,256,4,128]{3,2,0,1:T(4,128)(2,1)S(1)}, u32[]{:S(2)}, u32[]{:S(2)}) async-start(bf16[2,256,4,128]{3,2,0,1:T(4,128)(2,1)} %get-tuple-element.80), calls=%async_computation.3 | async-start | bytes 1048576 | tf_op jit(solution)/shard_map/all_to_all | solution.py:93
  195.0 18.4 %copy-start.5 = (s32[2048,1]{0,1:T(1,128)S(1)}, s32[2048,1]{0,1:T(1,128)}, u32[]{:S(2)}) copy-start(s32[2048,1]{0,1:T(1,128)} %compare_select_fusion.1) | copy-start | bytes 24580
  198.4 48.0 %all-to-all-start.6 = ((s32[16,1,16]{2,1,0:T(1,128)}), s32[16,1,16]{2,1,0:T(1,128)S(1)}, u32[]{:S(2)}, u32[]{:S(2)}) async-start(s32[16,1,16]{2,1,0:T(1,128)} %all_to_all.84), calls=%async_computation.6 | async-start | bytes 16384 | tf_op jit(solution)/shard_map/all_to_all | solution.py:109
  246.4 188.6 %all-to-all-start.4 = ((bf16[16,256,1024]{2,1,0:T(8,128)(2,1)}), bf16[16,256,1024]{2,1,0:T(8,128)(2,1)}, u32[]{:S(2)}, u32[]{:S(2)}) async-start(bf16[16,256,1024]{2,1,0:T(8,128)(2,1)} %bitcast.189), calls=%async_computation.4 | async-start | bytes 16777216 | tf_op jit(solution)/shard_map/all_to_all | solution.py:139
  435.0 97.4 %all-to-all-start.7 = ((bf16[16,16,4,16,128]{4,3,2,1,0:T(8,128)(2,1)}), bf16[16,16,4,16,128]{4,3,2,1,0:T(8,128)(2,1)}, u32[]{:S(2)}, u32[]{:S(2)}) async-start(bf16[16,16,4,16,128]{4,3,2,1,0:T(8,128)(2,1)} %bitcast.192), calls=%async_computation.7 | async-start | bytes 8388608 | tf_op jit(solution)/shard_map/all_to_all | solution.py:108
  439.9 46.9 %all-gather.2.cloned.1.call-start = ((), (), s32[]{:S(2)}) async-start(), calls=%async_computation.8 | async-start | bytes 4718592 | tf_op jit(solution)/shard_map/all_gather | solution.py:138
  514.2 23.5 %copy-start.6 = (f32[256,8]{0,1:T(8,128)S(1)}, f32[256,8]{0,1:T(8,128)}, u32[]{:S(2)}) copy-start(f32[256,8]{0,1:T(8,128)} %param.23) | copy-start | bytes 24580
  532.4 187.5 %all-to-all-start.5 = ((bf16[16,256,1024]{2,1,0:T(8,128)(2,1)}), bf16[16,256,1024]{2,1,0:T(8,128)(2,1)}, u32[]{:S(2)}, u32[]{:S(2)}) async-start(bf16[16,256,1024]{2,1,0:T(8,128)(2,1)} %convolution_convert_fusion), calls=%async_computation.5 | async-start | bytes 16777216 | tf_op jit(solution)/shard_map/all_to_all | solution.py:152
Sparse Core Ops, SparseCore 0:
  442.3 44.5 all-gather.1
where the time goes:
time: 760 us; the launch traced here: 748 us
  waiting for transfers between devices  417 us (55%)
  local copies, waits for them, and re-layouts  147 us (19%)
  other arithmetic  68.1 us (9%)
  matrix products  58.8 us (8%)
  starting transfers between devices  43.5 us (6%)
  between operations  14.8 us (2%)
    all_to_all x1, waiting for transfers between devices, body(): lax.all_to_all(buffer, 'req', split_axis=0, concat_axis=0, tiled=True)  170 us
    all_to_all x1, waiting for transfers between devices, body(): lax.all_to_all(expert_out.reshape(slot_block.shape), 'req', split_axis=0,...  144 us
    all_gather x1, waiting for transfers between devices, body(): full_weights = lax.all_gather(w_experts, 'kv', axis=3, tiled=True)  46.2 us
    sub x2, other arithmetic, soft_weights(): probability = jnp.where(allowed, jnp.exp(masked - row_max), 0.0)  38.9 us
    scatter x1, local copies, waits for them, and re-layouts, body(): decode_pool = jnp.zeros((slots_dev, group_count, BLOCK, head_pair), jnp.b...  33.5 us
    scatter x1, local copies, waits for them, and re-layouts, body(): buffer = jnp.zeros((experts * capacity, width_model), jnp.bfloat16).at[ta...  33 us
    all_to_all x1, waiting for transfers between devices, body(): lax.all_to_all(cache, 'kv', split_axis=2, concat_axis=1, tiled=True)  28.7 us
    dynamic_slice x10, local copies, waits for them, and re-layouts, body(): lax.map(whole_request, (query_heads, cache_heads, span_heads, lengths))  20.2 us
  transfers between devices with their start and end apart: 9, of which 8 were waited for; matrix products, arithmetic and copies ran while one was open for 19% of the time, Pallas kernels for 0%

commit v1 on v0

--- a/solution.py
+++ b/solution.py
@@ -85,7 +85,10 @@
     lengths = lookup_lengths(req_order, cached_len, local_reqs)
     queries_grouped = queries.reshape(local_reqs, local_tokens, kv_heads, group_width)
     cache_heads, span_heads, query_heads = (
-        lax.all_to_all(cache, "kv", split_axis=2, concat_axis=1, tiled=True),
+        jnp.concatenate(
+            lax.all_to_all(jnp.stack(jnp.split(cache, lax.axis_size("kv"), axis=2)), "kv", 0, 0),
+            axis=1,
+        ),
         lax.all_to_all(span_kv, "kv", split_axis=2, concat_axis=1, tiled=True),
         lax.all_to_all(queries_grouped, "kv", split_axis=2, concat_axis=1, tiled=True),
     )

time: 760 us -> 759 us (level)
  transfers between devices with their start and end apart: 9 -> 9, of which waited for: 8 -> 6; matrix products, arithmetic and copies ran while one was open for 19% -> 20% of each run, Pallas kernels for 0% -> 0%
where the time goes in v1:
time: 759 us; the launch traced here: 754 us
  waiting for transfers between devices  413 us (54%)
  local copies, waits for them, and re-layouts  153 us (20%)
  other arithmetic  72.7 us (10%)
  matrix products  58.8 us (8%)
  starting transfers between devices  42.1 us (6%)
  between operations  14.6 us (2%)
    all_to_all x1, waiting for transfers between devices, body(): lax.all_to_all(buffer, 'req', split_axis=0, concat_axis=0, tiled=True)  170 us
    all_to_all x1, waiting for transfers between devices, body(): lax.all_to_all(expert_out.reshape(slot_block.shape), 'req', split_axis=0,...  144 us
    all_gather x1, waiting for transfers between devices, body(): full_weights = lax.all_gather(w_experts, 'kv', axis=3, tiled=True)  46.2 us
    sub x2, other arithmetic, soft_weights(): probability = jnp.where(allowed, jnp.exp(masked - row_max), 0.0)  38.9 us
    scatter x1, local copies, waits for them, and re-layouts, body(): decode_pool = jnp.zeros((slots_dev, group_count, BLOCK, head_pair), jnp.b...  33.5 us
    scatter x1, local copies, waits for them, and re-layouts, body(): buffer = jnp.zeros((experts * capacity, width_model), jnp.bfloat16).at[ta...  33 us
    all_to_all x1, waiting for transfers between devices, body(): lax.all_to_all(jnp.stack(jnp.split(cache, lax.axis_size('kv'), axis=2)),...  30.5 us
    dynamic_slice x10, local copies, waits for them, and re-layouts, body(): lax.map(whole_request, (query_heads, cache_heads, span_heads, lengths))  20.2 us
  transfers between devices with their start and end apart: 9, of which 6 were waited for; matrix products, arithmetic and copies ran while one was open for 20% of the time, Pallas kernels for 0%

profile of v1, /device:TPU:11, one launch (start us, length us, event | category | flops | bytes accessed | tf_op | source)
XLA Modules:
  0.0 754.5 jit_solution(14967789713718527178)
XLA Ops:
  7.2 2.1 copy.67
  9.3 3.5 all-to-all-start.1
  12.8 6.3 fusion.47
  19.1 1.3 copy.69
  20.4 0.8 copy.70
  21.3 3.5 all-to-all-start.2
  24.8 5.1 copy_bitcast_fusion
  30.2 4.6 pad_maximum_fusion
  34.9 6.3 all-to-all-start
  41.2 4.5 reduce-window.6
  47.3 3.2 sort.17
  53.2 1.1 copy.68
  54.3 2.2 all_to_all.59
  56.4 1.0 copy.72
  57.5 30.5 %all-to-all-done = bf16[2,2,1024,4,128]{4,2,3,1,0:T(8,128)(2,1)} async-done(((bf16[2,2,1024,4,128]{4,2,3,1,0:T(8,128)(2,1)}), bf16[2,2,1024,4,128]{4,2,3,1,0:T(8,128)(2,1)}, u32[]{:S(2)}, u32[]{:S(2)}) %all-to-all-start) | async-done | bytes 4194336 | tf_op jit(solution)/shard_map/all_to_all | solution.py:89
  87.9 4.6 copy.66
  92.5 104.1 %while.12 = (s32[]{:T(128)}, bf16[2,256,4,128]{3,2,0,1:T(4,128)(2,1)}, bf16[2,2048,4,128]{3,1,2,0:T(8,128)(2,1)}, bf16[2,256,4,128]{1,3,2,0:T(8,128)(2,1)}, s32[...) while((s32[]{:T(128)}, bf16[2,256,4,128]{3,2,0,1:T(4,128)(2,1)}, ...), condition=%wide.region_4.5_spmd, body=%wide.region_1.4_spmd.sunk | while | flops 1251877888 | bytes 80653984 | solution.py:95
  92.5 3.0 constant_dynamic-slice_fusion.5
  95.6 4.0 copy.102
  99.6 2.8 fusion.65
  103.1 0.7 constant_dynamic-slice_fusion.4
  103.8 1.1 copy.101
  104.9 9.2 %fusion.66 = f32[4,2304,256,2]{2,1,3,0:T(8,128)} fusion(bf16[256,4,2,64]{0,3,2,1:T(8,128)(2,1)S(1)} %bitcast.192, bf16[256,4,64]{0,2,1:T(8,128)(2,1)} %get-tuple-element.181, bf16[2048,4,64]{0,2,1:T(8,128)(2,1)} %get-tuple-element.182), kind=kOutput, calls=%fused_computation.24.clone.1 | convolution fusion | flops 606339072 | bytes 20316160 | tf_op jit(solution)/shard_map/while/body/eval_jaxpr/igsd,pgd->gsip/dot_general | solution.py:24
  114.1 1.2 dynamic_slice.41
  116.0 2.7 fusion.67
  118.7 19.4 %fusion.68 = (f32[4,2,256]{2,1,0:T(2,128)S(1)}, bf16[4,2,256,2304]{2,3,1,0:T(8,128)(2,1)}) fusion(f32[4,2304,256,2]{2,1,3,0:T(8,128)} %fusion.66, pred[256,2304]{0,1:T(8,128)(4,1)} %fusion.67), kind=kOutput, calls=%fused_computation.102.clone.1 | output fusion | flops 37751040 | bytes 28909568 | tf_op jit(solution)/shard_map/while/body/eval_jaxpr/sub | solution.py:33
  138.2 5.5 fusion.69
  143.8 0.8 constant_dynamic-update-slice_fusion.2
  144.6 3.0 constant_dynamic-slice_fusion.5
  147.6 4.0 copy.102
  151.6 2.8 fusion.65
  155.1 0.7 constant_dynamic-slice_fusion.4
  155.9 1.1 copy.101
  157.0 9.2 %fusion.66 = f32[4,2304,256,2]{2,1,3,0:T(8,128)} fusion(bf16[256,4,2,64]{0,3,2,1:T(8,128)(2,1)S(1)} %bitcast.192, bf16[256,4,64]{0,2,1:T(8,128)(2,1)} %get-tuple-element.181, bf16[2048,4,64]{0,2,1:T(8,128)(2,1)} %get-tuple-element.182), kind=kOutput, calls=%fused_computation.24.clone.1 | convolution fusion | flops 606339072 | bytes 20316160 | tf_op jit(solution)/shard_map/while/body/eval_jaxpr/igsd,pgd->gsip/dot_general | solution.py:24
  166.2 1.2 dynamic_slice.41
  168.1 2.7 fusion.67
  170.8 19.4 %fusion.68 = (f32[4,2,256]{2,1,0:T(2,128)S(1)}, bf16[4,2,256,2304]{2,3,1,0:T(8,128)(2,1)}) fusion(f32[4,2304,256,2]{2,1,3,0:T(8,128)} %fusion.66, pred[256,2304]{0,1:T(8,128)(4,1)} %fusion.67), kind=kOutput, calls=%fused_computation.102.clone.1 | output fusion | flops 37751040 | bytes 28909568 | tf_op jit(solution)/shard_map/while/body/eval_jaxpr/sub | solution.py:33
  190.2 5.5 fusion.69
  195.9 0.8 constant_dynamic-update-slice_fusion.2
  196.7 3.6 all-to-all-start.3
  200.3 1.9 gather_fusion.1
  203.7 3.1 all-to-all-done.3
  206.8 8.6 %all-to-all-start.6 = ((s32[16,1,16]{2,1,0:T(1,128)}), s32[16,1,16]{2,1,0:T(1,128)S(1)}, u32[]{:S(2)}, u32[]{:S(2)}) async-start(s32[16,1,16]{2,1,0:T(1,128)} %all_to_all.69), calls=%async_computation.6 | async-start | bytes 16384 | tf_op jit(solution)/shard_map/all_to_all | solution.py:112
  215.6 1.2 reshape.277
  216.7 2.0 multiply_reduce_fusion
  218.7 0.9 multiply_convert_fusion
  219.7 33.0 %scatter_custom_fusion = bf16[4096,1024]{1,0:T(8,128)(2,1)} fusion(s32[2048]{0:T(1024)S(1)} %bitcast.207, bf16[256,1024]{1,0:T(8,128)(2,1)} %multiply_convert_fusion, s32[2048]{0:T(1024)S(1)} %broadcast_clamp_fusion.1, bf16[]{:T(256)} %constant.114.clone.1), kind=kCustom, calls=%fused_computation.50 | custom fusion | bytes 8389120 | tf_op jit(solution)/shard_map/scatter | solution.py:138
  252.7 6.4 all-to-all-start.4
  259.8 2.6 select_bitcast_fusion
  262.4 3.3 copy.81
  265.7 5.2 gather_fusion.2
  270.9 170.4 %all-to-all-done.4 = bf16[16,256,1024]{2,1,0:T(8,128)(2,1)} async-done(((bf16[16,256,1024]{2,1,0:T(8,128)(2,1)}), bf16[16,256,1024]{2,1,0:T(8,128)(2,1)}, u32[]{:S(2)}, u32[]{:S(2)}) %all-to-all-start.4) | async-done | bytes 8388640 | tf_op jit(solution)/shard_map/all_to_all | solution.py:142
  441.3 4.9 all-to-all-start.7
  446.9 46.2 %all-gather.2.cloned.1.call-done = bf16[1,3,1024,512]{3,2,1,0:T(8,128)(2,1)} async-done(((bf16[1,3,1024,256]{3,2,1,0:T(8,128)(2,1)}), bf16[1,3,1024,512]{3,2,1,0:T(8,128)(2,1)}) %all-gather.2.cloned.1.call-update) | async-done | bytes 3145744 | tf_op jit(solution)/shard_map/all_gather | solution.py:141
  493.1 11.4 %fusion.38 = f32[16,256,512]{2,1,0:T(8,128)} fusion(bf16[16,256,1024]{2,1,0:T(8,128)(2,1)} %all-to-all-done.4, bf16[1,3,1024,512]{3,2,1,0:T(8,128)(2,1)} %all-gather.2.cloned.1.call-done), kind=kOutput, calls=%fused_computation.61 | convolution fusion | flops 4294967296 | bytes 17825792 | tf_op jit(solution)/shard_map/sejd,edf->sejf/dot_general | solution.py:145
  504.4 16.0 %convolution_convert_fusion = bf16[16,256,1024]{2,1,0:T(8,128)(2,1)} fusion(f32[16,256,512]{2,1,0:T(8,128)} %fusion.38, bf16[16,256,1024]{2,1,0:T(8,128)(2,1)} %all-to-all-done.4, bf16[1,3,1024,512]{3,2,1,0:T(8,128)(2,1)} %all-gather.2.cloned.1.call-done), kind=kOutput, calls=%fused_computation.47 | convolution fusion | flops 8606711808 | bytes 27262976 | tf_op jit(solution)/shard_map/sejf,edf->sejd/dot_general | solution.py:152
  520.4 18.2 %all-to-all-done.7 = bf16[16,16,4,16,128]{4,3,2,1,0:T(8,128)(2,1)} async-done(((bf16[16,16,4,16,128]{4,3,2,1,0:T(8,128)(2,1)}), bf16[16,16,4,16,128]{4,3,2,1,0:T(8,128)(2,1)}, u32[]{:S(2)}, u32[]{:S(2)}) %all-to-all-start.7) | async-done | bytes 4194336 | tf_op jit(solution)/shard_map/all_to_all | solution.py:111
  538.6 5.3 all-to-all-start.5
  545.4 3.1 broadcast_in_dim.106
  548.4 33.5 %scatter_fusion = bf16[256,4,16,128]{3,2,1,0:T(8,128)(2,1)} fusion(bf16[256,4,16,128]{3,2,1,0:T(8,128)(2,1)} %broadcast_in_dim.106, s32[256]{0:T(256)S(1)} %bitcast.211, bf16[256,4,16,128]{3,2,1,0:T(8,128)(2,1)} %bitcast.55), kind=kCustom, calls=%fused_computation.5 | custom fusion | bytes 12583936 | tf_op jit(solution)/shard_map/scatter | solution.py:119
  581.9 144.2 %all-to-all-done.5 = bf16[16,256,1024]{2,1,0:T(8,128)(2,1)} async-done(((bf16[16,256,1024]{2,1,0:T(8,128)(2,1)}), bf16[16,256,1024]{2,1,0:T(8,128)(2,1)}, u32[]{:S(2)}, u32[]{:S(2)}) %all-to-all-start.5) | async-done | bytes 8388640 | tf_op jit(solution)/shard_map/all_to_all | solution.py:155
  726.1 15.5 %gather_fusion = bf16[2048,1024]{1,0:T(8,128)(2,1)} fusion(bf16[4096,1024]{1,0:T(8,128)(2,1)} %bitcast.46, s32[2048]{0:T(1024)S(1)} %broadcast_clamp_fusion), kind=kCustom, calls=%fused_computation.1 | custom fusion | bytes 8396800 | tf_op jit(solution)/shard_map/gather | solution.py:158
  741.6 4.8 fusion.26
  746.4 1.0 add_convert_fusion
  (75 shorter events, 12.0 us)
Async XLA Ops:
  7.2 209.5 %copy-start = (bf16[1024,1024]{1,0:T(8,128)(2,1)S(1)}, bf16[1024,1024]{1,0:T(8,128)(2,1)}, u32[]{:S(2)}) copy-start(bf16[1024,1024]{1,0:T(8,128)(2,1)} %param.20) | copy-start | bytes 6291460
  9.3 12.0 %all-to-all-start.1 = ((bf16[2,128,8,128]{3,1,0,2:T(8,128)(2,1)}), bf16[2,128,8,128]{3,1,0,2:T(8,128)(2,1)S(1)}, u32[]{:S(2)}, u32[]{:S(2)}) async-start(bf16[2,128,8,128]{3,1,0,2:T(8,128)(2,1)} %copy.67), calls=%async_computation.1 | async-start | bytes 1048576 | tf_op jit(solution)/shard_map/all_to_all | solution.py:92
  21.3 13.6 %all-to-all-start.2 = ((bf16[2,128,8,128]{1,3,0,2:T(8,128)(2,1)}), bf16[2,128,8,128]{1,3,0,2:T(8,128)(2,1)S(1)}, u32[]{:S(2)}, u32[]{:S(2)}) async-start(bf16[2,128,8,128]{1,3,0,2:T(8,128)(2,1)} %copy.70), calls=%async_computation.2 | async-start | bytes 1048576 | tf_op jit(solution)/shard_map/all_to_all | solution.py:93
  24.8 5.1 copy-start.4
  34.9 11.7 %copy-start.10 = (s32[32]{0:T(128)S(1)}, s32[32]{0:T(128)}, u32[]{:S(2)}) copy-start(s32[32]{0:T(128)} %param.18) | copy-start | bytes 388
  34.9 11.8 %copy-start.9 = (s32[2,128]{1,0:T(2,128)S(1)}, s32[2,128]{1,0:T(2,128)}, u32[]{:S(2)}) copy-start(s32[2,128]{1,0:T(2,128)} %param.25) | copy-start | bytes 3076
  34.9 15.6 %copy-start.11 = (s32[32]{0:T(128)S(1)}, s32[32]{0:T(128)}, u32[]{:S(2)}) copy-start(s32[32]{0:T(128)} %param.19) | copy-start | bytes 388
  34.9 53.1 %all-to-all-start = ((bf16[2,2,1024,4,128]{4,2,3,1,0:T(8,128)(2,1)}), bf16[2,2,1024,4,128]{4,2,3,1,0:T(8,128)(2,1)}, u32[]{:S(2)}, u32[]{:S(2)}) async-start(bf16[2,2,1024,4,128]{4,2,3,1,0:T(8,128)(2,1)} %pad_maximum_fusion), calls=%async_computation | async-start | bytes 8388608 | tf_op jit(solution)/shard_map/all_to_all | solution.py:89
  92.5 107.8 %copy-start.8 = (s32[256]{0:T(256)S(1)}, s32[256]{0:T(256)}, u32[]{:S(2)}) copy-start(s32[256]{0:T(256)} %compare_select_fusion.3) | copy-start | bytes 3076
  92.5 107.8 %copy-start.1 = (s32[256]{0:T(256)S(1)}, s32[256]{0:T(256)}, u32[]{:S(2)}) copy-start(s32[256]{0:T(256)} %get-tuple-element.129) | copy-start | bytes 3076
  99.6 2.8 copy-start.2
  99.6 3.5 copy-start.3
  151.6 2.8 copy-start.2
  151.6 3.5 copy-start.3
  196.7 22.1 %copy-start.7 = (f32[1024]{0:T(1024)S(1)}, f32[1024]{0:T(1024)}, u32[]{:S(2)}) copy-start(f32[1024]{0:T(1024)} %param.21) | copy-start | bytes 12292
  196.7 10.1 %all-to-all-start.3 = ((bf16[2,256,4,128]{3,2,0,1:T(4,128)(2,1)}), bf16[2,256,4,128]{3,2,0,1:T(4,128)(2,1)S(1)}, u32[]{:S(2)}, u32[]{:S(2)}) async-start(bf16[2,256,4,128]{3,2,0,1:T(4,128)(2,1)} %get-tuple-element.80), calls=%async_computation.3 | async-start | bytes 1048576 | tf_op jit(solution)/shard_map/all_to_all | solution.py:96
  202.3 17.4 %copy-start.5 = (s32[2048,1]{0,1:T(1,128)S(1)}, s32[2048,1]{0,1:T(1,128)}, u32[]{:S(2)}) copy-start(s32[2048,1]{0,1:T(1,128)} %compare_select_fusion.1) | copy-start | bytes 24580
  206.8 45.9 %all-to-all-start.6 = ((s32[16,1,16]{2,1,0:T(1,128)}), s32[16,1,16]{2,1,0:T(1,128)S(1)}, u32[]{:S(2)}, u32[]{:S(2)}) async-start(s32[16,1,16]{2,1,0:T(1,128)} %all_to_all.69), calls=%async_computation.6 | async-start | bytes 16384 | tf_op jit(solution)/shard_map/all_to_all | solution.py:112
  252.7 188.6 %all-to-all-start.4 = ((bf16[16,256,1024]{2,1,0:T(8,128)(2,1)}), bf16[16,256,1024]{2,1,0:T(8,128)(2,1)}, u32[]{:S(2)}, u32[]{:S(2)}) async-start(bf16[16,256,1024]{2,1,0:T(8,128)(2,1)} %bitcast.191), calls=%async_computation.4 | async-start | bytes 16777216 | tf_op jit(solution)/shard_map/all_to_all | solution.py:142
  441.3 97.4 %all-to-all-start.7 = ((bf16[16,16,4,16,128]{4,3,2,1,0:T(8,128)(2,1)}), bf16[16,16,4,16,128]{4,3,2,1,0:T(8,128)(2,1)}, u32[]{:S(2)}, u32[]{:S(2)}) async-start(bf16[16,16,4,16,128]{4,3,2,1,0:T(8,128)(2,1)} %bitcast.194), calls=%async_computation.7 | async-start | bytes 8388608 | tf_op jit(solution)/shard_map/all_to_all | solution.py:111
  446.1 46.9 %all-gather.2.cloned.1.call-start = ((), (), s32[]{:S(2)}) async-start(), calls=%async_computation.8 | async-start | bytes 4718592 | tf_op jit(solution)/shard_map/all_gather | solution.py:141
  520.4 23.5 %copy-start.6 = (f32[256,8]{0,1:T(8,128)S(1)}, f32[256,8]{0,1:T(8,128)}, u32[]{:S(2)}) copy-start(f32[256,8]{0,1:T(8,128)} %param.23) | copy-start | bytes 24580
  538.6 187.5 %all-to-all-start.5 = ((bf16[16,256,1024]{2,1,0:T(8,128)(2,1)}), bf16[16,256,1024]{2,1,0:T(8,128)(2,1)}, u32[]{:S(2)}, u32[]{:S(2)}) async-start(bf16[16,256,1024]{2,1,0:T(8,128)(2,1)} %convolution_convert_fusion), calls=%async_computation.5 | async-start | bytes 16777216 | tf_op jit(solution)/shard_map/all_to_all | solution.py:155
Sparse Core Ops, SparseCore 0:
  448.5 44.5 all-gather.1
